TPU v7x, 32 devices: a whole 2x2x4 slice. The times are simulated.
32 devices in a mesh: lon: 4 (over x, core), lat: 8 (over z, y).
Axes of the slice: x: 2, y: 2, z: 4, core: 2. Of those that a mesh axis runs over, the one named last changes fastest.
Arguments:
- prognostic: float32 [4, 16, 192, 1536], P(None, None, 'lat', 'lon'), may hold values from -6 to 6
- tracers: float32 [4, 16, 192, 1536], P(None, None, 'lat', 'lon'), may hold values from -6 to 6
- zonal_courant: float32 [16, 192, 1536], P(None, 'lat', 'lon'), may hold values from -0.45 to 0.45
- meridional_courant: float32 [16, 192, 1536], P(None, 'lat', 'lon'), may hold values from -0.45 to 0.45
- filter_band: int32 [192], P('lat'), may hold values from 96 to 768, as said below
- dep_owner: int32 [192, 2], P('lat'), may hold values from 0 to 7, as said below
- dep_row: int32 [192, 2], P('lat'), may hold values from 0 to 23
- dep_weight: float32 [192, 2], P('lat'), may hold values from 0 to 1, as said below
Outputs:
- new_prognostic: float32 [4, 16, 192, 1536], P(None, None, 'lat', 'lon')
- new_tracers: float32 [4, 16, 192, 1536], P(None, None, 'lat', 'lon')
Inputs may be any that keep to these rules, and one draw needn't show every extreme that they name: `filter_band`: rows within 24 of either pole hold values below 768; all other rows hold 768. `dep_owner`: among the 48 entries of one band, at most 12 name the same owner band, and some owner is named exactly 12 times; the owners a band names are the bands nearest to it, distance counted across either pole. `dep_weight`: Positive; the 2 weights of a row sum to 1.
All inputs are finite; a program needn't handle non-finite values.
Results may differ from a plain program's by a relative error of at most 0.00007.
Values sent between devices are 32-bit elements; how exact they have to be, the bound alone decides.
No kernel may reach another device: no remote copies, remote signals or barrier semaphores. Data moves between devices by JAX's collectives and lax.ppermute only.
A program may use at most 128 MiB of HBM per device.

v0:
```python
import math
import jax
import jax.numpy as jnp
from jax import lax
from jax.sharding import PartitionSpec as P

PRECISE = lax.Precision.HIGHEST


def padded(value, sides, width, wrap):
    for axis, dim in sides:
        size, length = (lax.axis_size(axis), value.shape[dim])
        up = [(i, (i + 1) % size) for i in range(size if wrap else size - 1)]
        down = [(j, i) for i, j in up]
        last = lax.slice_in_dim(value, length - width, length, axis=dim)
        first = lax.slice_in_dim(value, 0, width, axis=dim)
        before = lax.ppermute(last, axis, up)
        after = lax.ppermute(first, axis, down)
        value = jnp.concatenate([before, value, after], axis=dim)
    return value


def face_flux(values, speeds, axis):
    count = values.shape[axis] - 2
    left_cells = lax.slice_in_dim(values, 0, count + 1, axis=axis)
    right_cells = lax.slice_in_dim(values, 1, count + 2, axis=axis)
    courant = lax.slice_in_dim(speeds, 0, count + 1, axis=axis)
    return 0.5 * courant * (left_cells + right_cells) - 0.5 * courant * courant * (
        right_cells - left_cells
    )


def column_factors(band_rows, length):
    column = jnp.arange(length, dtype=jnp.int32)
    half_length = length // 2
    frequency = jnp.where(column <= half_length, column, column - half_length)
    single = (column == 0) | (column == half_length)
    weights = jnp.where(single, 1.0 / length, 2.0 / length).astype(jnp.float32)
    ratios = (
        band_rows.astype(jnp.float32)[:, None]
        / jnp.maximum(frequency, 1).astype(jnp.float32)[None, :]
    )
    damping = jnp.minimum(1.0, ratios * ratios)
    return (damping - 1.0) * weights[None, :]


def circle_basis(length):
    half_length = length // 2
    column = jnp.arange(length, dtype=jnp.int32)
    frequency = jnp.where(column <= half_length, column, column - half_length)
    low_count = 64
    high_count = length // low_count
    low = jnp.arange(low_count, dtype=jnp.int32)
    high = jnp.arange(high_count, dtype=jnp.int32) * low_count
    scale = 2.0 * math.pi / length
    low_angle = scale * (low[:, None] * frequency[None, :] % length).astype(jnp.float32)
    high_angle = scale * (high[:, None] * frequency[None, :] % length).astype(jnp.float32)
    low_cos, low_sin = (jnp.cos(low_angle), jnp.sin(low_angle))
    high_cos, high_sin = (jnp.cos(high_angle), jnp.sin(high_angle))
    cos_part = high_cos[:, None] * low_cos[None] - high_sin[:, None] * low_sin[None]
    sin_part = high_sin[:, None] * low_cos[None] + high_cos[:, None] * low_sin[None]
    basis = jnp.where((column <= half_length)[None, None, :], cos_part, sin_part)
    return basis.reshape(length, length)


def polar_filter(values, band_rows):
    fields, levels, rows, block_cells = values.shape
    parts = lax.axis_size("lon")
    length = block_cells * parts
    flat = values.reshape(fields * levels * rows, block_cells)
    circles = lax.all_to_all(flat, "lon", split_axis=0, concat_axis=1, tiled=True)
    basis_table = circle_basis(length)
    spectrum = jnp.dot(circles, basis_table, precision=PRECISE)
    factors = column_factors(band_rows, length)
    circle_rows = circles.shape[0]
    scaled = (spectrum.reshape(circle_rows // rows, rows, length) * factors[None]).reshape(
        circle_rows, length
    )
    change = lax.dot_general(scaled, basis_table, (((1,), (1,)), ((), ())), precision=PRECISE)
    back = lax.all_to_all(change, "lon", split_axis=1, concat_axis=0, tiled=True)
    return values + back.reshape(values.shape)


def departure_terms(tracers, dep_owner, dep_row, dep_weight):
    band_count = lax.axis_size("lat")
    row_count, link_count = dep_owner.shape
    entries = row_count * link_count
    capacity = max(2, -(-2 * entries // band_count))
    owner_ids = dep_owner.reshape(entries)
    source = dep_row.reshape(entries)
    positions = jnp.arange(entries)
    earlier = (owner_ids[:, None] == owner_ids[None, :]) & (positions[None, :] < positions[:, None])
    slot_ids = jnp.sum(earlier.astype(jnp.int32), axis=1)
    band_ids = jnp.arange(band_count, dtype=jnp.int32)
    slot_range = jnp.arange(capacity, dtype=jnp.int32)
    matches = (owner_ids[:, None, None] == band_ids[None, :, None]) & (
        slot_ids[:, None, None] == slot_range[None, None, :]
    )
    request = jnp.sum(jnp.where(matches, source[:, None, None], 0), axis=0)
    wanted = lax.all_to_all(request, "lat", split_axis=0, concat_axis=0, tiled=True)
    by_row = jnp.transpose(tracers, (2, 0, 1, 3))
    outgoing = by_row[wanted]
    incoming = lax.all_to_all(outgoing, "lat", split_axis=0, concat_axis=0, tiled=True)
    stacked_rows = incoming.reshape((band_count * capacity,) + incoming.shape[2:])
    picked = stacked_rows[owner_ids * capacity + slot_ids].reshape(
        (row_count, link_count) + stacked_rows.shape[1:]
    )
    summed = dep_weight[:, 0][:, None, None, None] * picked[:, 0]
    summed = summed + dep_weight[:, 1][:, None, None, None] * picked[:, 1]
    return jnp.transpose(summed, (1, 2, 0, 3))


def body(
    prognostic,
    tracers,
    zonal_courant,
    meridional_courant,
    filter_band,
    dep_owner,
    dep_row,
    dep_weight,
):
    row_count = prognostic.shape[2]
    departed = departure_terms(tracers, dep_owner, dep_row, dep_weight)
    lon_padded = padded(
        jnp.concatenate([prognostic, zonal_courant[None]], axis=0), (("lon", 3),), 1, True
    )
    zonal_flux = face_flux(lon_padded[:-1], lon_padded[-1:], 3)
    lat_padded = padded(
        jnp.concatenate([prognostic, meridional_courant[None]], axis=0), (("lat", 2),), 1, False
    )
    merid_flux = face_flux(lat_padded[:-1], lat_padded[-1:], 2)
    total_rows = row_count * lax.axis_size("lat")
    face_rows = lax.axis_index("lat") * row_count + jnp.arange(row_count + 1) - 1
    merid_flux = jnp.where(
        (face_rows == total_rows - 1)[None, None, :, None], jnp.float32(0.0), merid_flux
    )
    advected = (
        prognostic
        - (zonal_flux[..., 1:] - zonal_flux[..., :-1])
        - (merid_flux[:, :, 1:] - merid_flux[:, :, :-1])
    )
    new_prognostic = polar_filter(advected, filter_band)
    return (new_prognostic, departed)


def solution(mesh):
    return jax.shard_map(
        body,
        mesh=mesh,
        in_specs=(
            P(None, None, "lat", "lon"),
            P(None, None, "lat", "lon"),
            P(None, "lat", "lon"),
            P(None, "lat", "lon"),
            P("lat"),
            P("lat", None),
            P("lat", None),
            P("lat", None),
        ),
        out_specs=(P(None, None, "lat", "lon"), P(None, None, "lat", "lon")),
        check_vma=False,
    )
```

profile of v0, /device:TPU:0, one launch (start us, length us, event | category | flops | bytes accessed | tf_op | source)
XLA Modules:
  0.0 364.4 jit_solution(3108932577473310589)
XLA Ops:
  0.7 3.3 pad_maximum_fusion.8
  4.0 1.8 copy.57
  5.7 0.5 collective-permute-start
  6.2 1.7 copy.59
  7.9 2.0 collective-permute-start.1
  9.9 0.2 pad_maximum_fusion.11
  10.1 0.7 copy.61
  10.8 4.9 %collective-permute-start.2 = (f32[5,16,1,384]{3,1,2,0:T(8,128)}, f32[5,16,1,384]{3,1,2,0:T(8,128)}, u32[]{:S(2)}, u32[]{:S(2)}) collective-permute-start(f32[5,16,1,384]{3,1,2,0:T(8,128)} %copy.61), channel_id=1, source_target_pairs={{0,1},{1,2},{2,3},{3,4},{4,5},{5,6},{6,7},{8,9},{9,10},{10,11},{11... | collective-permute-start | bytes 368648 | tf_op jit(solution)/shard_map/ppermute | solution.py:17
  15.6 0.7 copy.63
  16.3 1.3 collective-permute-start.3
  17.7 0.1 eq.83
  17.8 0.2 convert_reduce_fusion
  18.2 0.1 broadcast_in_dim.82
  18.3 0.3 copy-done.9
  18.6 0.1 fusion.18
  18.7 0.3 select_reduce_fusion
  19.0 0.6 add_compare_fusion
  19.5 1.3 copy.58
  20.8 2.2 multiply_bitcast_fusion.1
  23.1 1.0 fusion.7
  24.0 2.3 copy.60
  26.3 2.7 multiply_subtract_fusion
  29.1 1.0 copy.62
  30.1 0.2 multiply_bitcast_fusion
  30.4 1.0 copy.64
  31.4 1.2 subtract_select_fusion
  32.6 2.3 fusion.4
  34.9 3.6 all-to-all-start
  38.5 0.7 copy.70
  39.2 0.7 fusion.24
  39.9 1.6 fusion.14
  41.5 5.8 %add_select_fusion = f32[24,64,1536]{2,1,0:T(8,128)} fusion(f32[64,1536]{1,0:T(8,128)S(1)} %get-tuple-element.21, f32[24,1536]{1,0:T(8,128)S(1)} %get-tuple-element.19, f32[64,1536]{1,0:T(8,128)S(1)} %get-tuple-element.20, f32[24,1536]{1,0:T(8,128)S(1)} %get-tuple-element.18, pred[1536]{0:T(1024)(128)(4,1)S(1)} %iota_compare_fusion.4), kind=kLoop, calls=%fused_computation.2 | loop fusion | flops 16515072 | bytes 10520064 | tf_op jit(solution)/shard_map/jit(_where)/select_n | solution.py:62
  47.3 19.7 %all-to-all-done = f32[4,384,384]{2,1,0:T(8,128)S(1)} async-done(((f32[4,384,384]{2,1,0:T(8,128)}), f32[4,384,384]{2,1,0:T(8,128)S(1)}, u32[]{:S(2)}, u32[]{:S(2)}) %all-to-all-start) | async-done | bytes 2359328 | tf_op jit(solution)/shard_map/all_to_all | solution.py:71
  67.0 6.9 %all-to-all-start.2 = ((s32[8,1,12]{2,1,0:T(1,128)}), s32[8,1,12]{2,1,0:T(1,128)S(1)}, u32[]{:S(2)}, u32[]{:S(2)}) async-start(s32[8,1,12]{2,1,0:T(1,128)} %copy.70), calls=%async_computation.2 | async-start | bytes 8192 | tf_op jit(solution)/shard_map/all_to_all | solution.py:100
  73.9 2.9 copy.65
  76.9 2.7 dot_general.8
  79.6 14.7 %convolution_multiply_fusion = f32[16,24,1536]{2,1,0:T(8,128)S(1)} fusion(f32[16,24,1536]{2,1,0:T(8,128)S(1)} %dot_general.8, f32[1536,1536,1]{1,0,2:T(8,128)} %bitcast.64, f32[24,1536]{1,0:T(8,128)S(1)} %fusion.18), kind=kOutput, calls=%fused_computation.13 | convolution fusion | flops 10872225792 | bytes 14303232 | tf_op jit(solution)/shard_map/dot_general | solution.py:73
  94.3 13.0 %fusion.31 = f32[384,4,384]{2,0,1:T(8,128)} fusion(f32[384,1536,1]{1,0,2:T(8,128)S(1)} %bitcast.71, f32[4,384,1536]{2,1,0:T(8,128)S(1)} %bitcast.65), kind=kOutput, calls=%fused_computation.87 | convolution fusion | flops 10871635968 | bytes 14155776 | tf_op jit(solution)/shard_map/dot_general | solution.py:79
  107.3 4.8 %all-to-all-start.1 = ((f32[384,4,384]{2,0,1:T(8,128)}), f32[384,4,384]{2,0,1:T(8,128)}, u32[]{:S(2)}, u32[]{:S(2)}) async-start(f32[384,4,384]{2,0,1:T(8,128)} %fusion.31), calls=%async_computation.1 | async-start | bytes 4718592 | tf_op jit(solution)/shard_map/all_to_all | solution.py:80
  112.1 2.1 copy.78
  114.3 4.8 %gather_fusion = f32[96,4,16,384]{3,2,1,0:T(8,128)} fusion(f32[24,4,16,384]{3,2,1,0:T(8,128)S(1)} %bitcast.66, s32[1024]{0:T(1024)S(1)} %pad_clamp_fusion.1), kind=kCustom, calls=%fused_computation | custom fusion | bytes 18874752 | tf_op jit(solution)/shard_map/gather | solution.py:102
  119.1 21.3 %all-to-all-done.1 = f32[384,4,384]{2,0,1:T(8,128)} async-done(((f32[384,4,384]{2,0,1:T(8,128)}), f32[384,4,384]{2,0,1:T(8,128)}, u32[]{:S(2)}, u32[]{:S(2)}) %all-to-all-start.1) | async-done | bytes 2359328 | tf_op jit(solution)/shard_map/all_to_all | solution.py:80
  140.4 6.1 %all-to-all-start.3 = ((f32[8,12,4,16,384]{4,3,2,1,0:T(8,128)}), f32[8,12,4,16,384]{4,3,2,1,0:T(8,128)}, u32[]{:S(2)}, u32[]{:S(2)}) async-start(f32[8,12,4,16,384]{4,3,2,1,0:T(8,128)} %bitcast.67), calls=%async_computation.3 | async-start | bytes 18874368 | tf_op jit(solution)/shard_map/all_to_all | solution.py:103
  146.8 3.3 add.134
  150.1 201.9 %all-to-all-done.3 = f32[8,12,4,16,384]{4,3,2,1,0:T(8,128)} async-done(((f32[8,12,4,16,384]{4,3,2,1,0:T(8,128)}), f32[8,12,4,16,384]{4,3,2,1,0:T(8,128)}, u32[]{:S(2)}, u32[]{:S(2)}) %all-to-all-start.3) | async-done | bytes 9437216 | tf_op jit(solution)/shard_map/all_to_all | solution.py:103
  352.0 6.7 %gather_fusion.1 = f32[48,4,16,384]{3,2,1,0:T(8,128)} fusion(f32[96,4,16,384]{3,2,1,0:T(8,128)} %bitcast.20, s32[1024]{0:T(1024)S(1)} %pad_clamp_fusion), kind=kCustom, calls=%fused_computation.1 | custom fusion | bytes 9437376 | tf_op jit(solution)/shard_map/gather | solution.py:105
  358.7 2.9 fusion.2
  361.6 2.8 copy.73
  (48 shorter events, 0.6 us)
Async XLA Ops:
  0.6 9.3 %copy-start = (f32[4,16,24,384]{3,2,1,0:T(8,128)S(1)}, f32[4,16,24,384]{3,2,1,0:T(8,128)}, u32[]{:S(2)}) copy-start(f32[4,16,24,384]{3,2,1,0:T(8,128)} %param.8) | copy-start | bytes 7077892
  0.6 9.3 %copy-start.3 = (f32[16,24,384]{2,1,0:T(8,128)S(1)}, f32[16,24,384]{2,1,0:T(8,128)}, u32[]{:S(2)}) copy-start(f32[16,24,384]{2,1,0:T(8,128)} %param.11) | copy-start | bytes 1769476
  4.0 13.7 %copy-start.5 = (s32[24,2]{0,1:T(2,128)S(1)}, s32[24,2]{0,1:T(2,128)}, u32[]{:S(2)}) copy-start(s32[24,2]{0,1:T(2,128)} %param.13) | copy-start | bytes 580
  4.0 14.1 %copy-start.11 = (s32[24]{0:T(128)S(1)}, s32[24]{0:T(128)}, u32[]{:S(2)}) copy-start(s32[24]{0:T(128)} %param.12) | copy-start | bytes 292
  4.0 14.1 %copy-start.7 = (s32[24,2]{0,1:T(2,128)S(1)}, s32[24,2]{0,1:T(2,128)}, u32[]{:S(2)}) copy-start(s32[24,2]{0,1:T(2,128)} %param.14) | copy-start | bytes 580
  5.7 13.8 %collective-permute-start = (f32[5,16,24,1]{2,1,3,0:T(8,128)S(1)}, f32[5,16,24,1]{2,1,3,0:T(8,128)}, u32[]{:S(2)}, u32[]{:S(2)}) collective-permute-start(f32[5,16,24,1]{2,1,3,0:T(8,128)S(1)} %copy.57), channel_id=1, source_target_pairs={{0,8},{8,16},{16,24},{24,0},{1,9},{9,17},{17,25},{25,1},{2,10},{10... | collective-permute-start | bytes 23048 | tf_op jit(solution)/shard_map/ppermute | solution.py:17
  7.9 16.1 %collective-permute-start.1 = (f32[5,16,24,1]{2,1,3,0:T(8,128)S(1)}, f32[5,16,24,1]{2,1,3,0:T(8,128)}, u32[]{:S(2)}, u32[]{:S(2)}) collective-permute-start(f32[5,16,24,1]{2,1,3,0:T(8,128)S(1)} %copy.59), channel_id=1, source_target_pairs={{8,0},{16,8},{24,16},{0,24},{9,1},{17,9},{25,17},{1,25},{10,2},{18... | collective-permute-start | bytes 23048 | tf_op jit(solution)/shard_map/ppermute | solution.py:18
  10.8 18.3 %collective-permute-start.2 = (f32[5,16,1,384]{3,1,2,0:T(8,128)}, f32[5,16,1,384]{3,1,2,0:T(8,128)}, u32[]{:S(2)}, u32[]{:S(2)}) collective-permute-start(f32[5,16,1,384]{3,1,2,0:T(8,128)} %copy.61), channel_id=1, source_target_pairs={{0,1},{1,2},{2,3},{3,4},{4,5},{5,6},{6,7},{8,9},{9,10},{10,11},{11... | collective-permute-start | bytes 368648 | tf_op jit(solution)/shard_map/ppermute | solution.py:17
  16.3 14.1 %collective-permute-start.3 = (f32[5,16,1,384]{3,1,2,0:T(8,128)}, f32[5,16,1,384]{3,1,2,0:T(8,128)}, u32[]{:S(2)}, u32[]{:S(2)}) collective-permute-start(f32[5,16,1,384]{3,1,2,0:T(8,128)} %copy.63), channel_id=1, source_target_pairs={{1,0},{2,1},{3,2},{4,3},{5,4},{6,5},{7,6},{9,8},{10,9},{11,10},{12... | collective-permute-start | bytes 368648 | tf_op jit(solution)/shard_map/ppermute | solution.py:18
  18.0 0.6 copy-start.9
  26.3 3.8 %copy-start.4 = (f32[16,24,384]{2,1,0:T(8,128)S(1)}, f32[16,24,384]{2,1,0:T(8,128)}, u32[]{:S(2)}) copy-start(f32[16,24,384]{2,1,0:T(8,128)} %param.11) | copy-start | bytes 1769476
  30.1 1.3 copy-start.8
  34.9 32.1 %all-to-all-start = ((f32[4,384,384]{2,1,0:T(8,128)}), f32[4,384,384]{2,1,0:T(8,128)S(1)}, u32[]{:S(2)}, u32[]{:S(2)}) async-start(f32[4,384,384]{2,1,0:T(8,128)} %bitcast.68), calls=%async_computation | async-start | bytes 4718592 | tf_op jit(solution)/shard_map/all_to_all | solution.py:71
  67.0 40.3 %all-to-all-start.2 = ((s32[8,1,12]{2,1,0:T(1,128)}), s32[8,1,12]{2,1,0:T(1,128)S(1)}, u32[]{:S(2)}, u32[]{:S(2)}) async-start(s32[8,1,12]{2,1,0:T(1,128)} %copy.70), calls=%async_computation.2 | async-start | bytes 8192 | tf_op jit(solution)/shard_map/all_to_all | solution.py:100
  79.6 14.8 %copy-start.1 = (f32[24,64,1536]{2,1,0:T(8,128)S(1)}, f32[24,64,1536]{2,1,0:T(8,128)}, u32[]{:S(2)}) copy-start(f32[24,64,1536]{2,1,0:T(8,128)} %add_select_fusion) | copy-start | bytes 28311556
  107.3 33.1 %all-to-all-start.1 = ((f32[384,4,384]{2,0,1:T(8,128)}), f32[384,4,384]{2,0,1:T(8,128)}, u32[]{:S(2)}, u32[]{:S(2)}) async-start(f32[384,4,384]{2,0,1:T(8,128)} %fusion.31), calls=%async_computation.1 | async-start | bytes 4718592 | tf_op jit(solution)/shard_map/all_to_all | solution.py:80
  140.4 6.3 %copy-start.10 = (s32[48]{0:T(128)S(1)}, s32[48]{0:T(128)}, u32[]{:S(2)}) copy-start(s32[48]{0:T(128)} %copy-done.9) | copy-start | bytes 580
  140.4 6.4 %copy-start.6 = (f32[24,2]{0,1:T(2,128)S(1)}, f32[24,2]{0,1:T(2,128)}, u32[]{:S(2)}) copy-start(f32[24,2]{0,1:T(2,128)} %param.15) | copy-start | bytes 580
  140.4 6.4 %copy-start.2 = (f32[4,16,24,384]{3,2,1,0:T(8,128)S(1)}, f32[4,16,24,384]{3,2,1,0:T(8,128)}, u32[]{:S(2)}) copy-start(f32[4,16,24,384]{3,2,1,0:T(8,128)} %fusion.4) | copy-start | bytes 7077892
  140.4 211.6 %all-to-all-start.3 = ((f32[8,12,4,16,384]{4,3,2,1,0:T(8,128)}), f32[8,12,4,16,384]{4,3,2,1,0:T(8,128)}, u32[]{:S(2)}, u32[]{:S(2)}) async-start(f32[8,12,4,16,384]{4,3,2,1,0:T(8,128)} %bitcast.67), calls=%async_computation.3 | async-start | bytes 18874368 | tf_op jit(solution)/shard_map/all_to_all | solution.py:103
where the time goes:
time: 365 us; the launch traced here: 364 us
  waiting for transfers between devices  243 us (67%)
  local copies, waits for them, and re-layouts  34.2 us (9%)
  starting transfers between devices  30.1 us (8%)
  other arithmetic  28.6 us (8%)
  matrix products  27.7 us (8%)
    all_to_all x1, waiting for transfers between devices, departure_terms(): lax.all_to_all(outgoing, 'lat', split_axis=0, concat_axis=0, tiled=True)  202 us
    all_to_all x1, waiting for transfers between devices, polar_filter(): lax.all_to_all(change, 'lon', split_axis=1, concat_axis=0, tiled=True)  21.3 us
    all_to_all x1, waiting for transfers between devices, polar_filter(): lax.all_to_all(flat, 'lon', split_axis=0, concat_axis=1, tiled=True)  19.7 us
    dot_general x1, matrix products, polar_filter(): spectrum = jnp.dot(circles, basis_table, precision=PRECISE)  14.7 us
    dot_general x1, matrix products, polar_filter(): lax.dot_general(scaled, basis_table, (((1,), (1,)), ((), ())), precision=...  13 us
  transfers between devices with their start and end apart: 8, of which 3 were waited for; matrix products, arithmetic and copies ran while one was open for 19% of the time, Pallas kernels for 0%

commit v1 on v0

--- a/solution.py
+++ b/solution.py
@@ -82,6 +82,29 @@
 
 
 def departure_terms(tracers, dep_owner, dep_row, dep_weight):
+
+    def scales_attach(packet):
+        dev_axis = "lat"
+        left_arr = lax.axis_size(dev_axis)
+        e_now, v1 = (left_arr, lax.axis_index(dev_axis))
+        value_now = list(packet.shape)
+        r2 = packet.shape[0] // e_now
+        value_now[0] = r2
+        arr_now = value_now[0]
+        value_now[0] = arr_now * e_now
+        current_value = jnp.zeros(value_now, packet.dtype)
+        for src_i in range(e_now):
+            r_now = lax.dynamic_slice_in_dim(packet, (v1 ^ src_i) * r2, r2, axis=0)
+            if src_i:
+                items = []
+                for u in range(e_now):
+                    items.append((u, u ^ src_i))
+                r_now = lax.ppermute(r_now, axis_name=dev_axis, perm=items)
+            current_value = lax.dynamic_update_slice_in_dim(
+                current_value, r_now, (v1 ^ src_i) * arr_now, axis=0
+            )
+        return current_value
+
     band_count = lax.axis_size("lat")
     row_count, link_count = dep_owner.shape
     entries = row_count * link_count
@@ -97,7 +120,7 @@
         slot_ids[:, None, None] == slot_range[None, None, :]
     )
     request = jnp.sum(jnp.where(matches, source[:, None, None], 0), axis=0)
-    wanted = lax.all_to_all(request, "lat", split_axis=0, concat_axis=0, tiled=True)
+    wanted = scales_attach(request)
     by_row = jnp.transpose(tracers, (2, 0, 1, 3))
     outgoing = by_row[wanted]
     incoming = lax.all_to_all(outgoing, "lat", split_axis=0, concat_axis=0, tiled=True)

time: 365 us -> 358 us (0.981)
  waiting for transfers between devices: 243 us -> 230 us
  starting transfers between devices: 30.1 us -> 36.8 us
    all_to_all x1, waiting for transfers between devices: 21.3 us -> 1.29 us  [polar_filter(): lax.all_to_all(change, 'lon', split_axis=1, concat_axis=0, tiled=True)]
    ppermute x0 -> x7, starting transfers between devices: none -> 12.5 us  [scales_attach(): r_now = lax.ppermute(r_now, axis_name=dev_axis, perm=items)]
    all_to_all x1 -> x0, starting transfers between devices: 6.94 us -> none  [departure_terms(): lax.all_to_all(request, 'lat', split_axis=0, concat_axis=0, tiled=True)]
    ppermute x0 -> x7, waiting for transfers between devices: none -> 5.53 us  [scales_attach(): r_now = lax.ppermute(r_now, axis_name=dev_axis, perm=items)]
  transfers between devices with their start and end apart: 8 -> 14, of which waited for: 3 -> 6; matrix products, arithmetic and copies ran while one was open for 19% -> 10% of each run, Pallas kernels for 0% -> 0%
where the time goes in v1:
time: 358 us; the launch traced here: 357 us
  waiting for transfers between devices  230 us (64%)
  starting transfers between devices  36.8 us (10%)
  local copies, waits for them, and re-layouts  33.6 us (9%)
  other arithmetic  27.7 us (8%)
  matrix products  27.7 us (8%)
    all_to_all x1, waiting for transfers between devices, departure_terms(): lax.all_to_all(outgoing, 'lat', split_axis=0, concat_axis=0, tiled=True)  202 us
    all_to_all x1, waiting for transfers between devices, polar_filter(): lax.all_to_all(flat, 'lon', split_axis=0, concat_axis=1, tiled=True)  20.2 us
    dot_general x1, matrix products, polar_filter(): spectrum = jnp.dot(circles, basis_table, precision=PRECISE)  14.7 us
    dot_general x1, matrix products, polar_filter(): lax.dot_general(scaled, basis_table, (((1,), (1,)), ((), ())), precision=...  13 us
    ppermute x7, starting transfers between devices, scales_attach(): r_now = lax.ppermute(r_now, axis_name=dev_axis, perm=items)  12.5 us
  transfers between devices with their start and end apart: 14, of which 6 were waited for; matrix products, arithmetic and copies ran while one was open for 10% of the time, Pallas kernels for 0%

profile of v1, /device:TPU:0, one launch (start us, length us, event | category | flops | bytes accessed | tf_op | source)
XLA Modules:
  0.0 357.1 jit_solution(9751716284253255025)
XLA Ops:
  0.7 1.9 pad_maximum_fusion.11
  2.5 0.6 copy.59
  3.2 5.5 %collective-permute-start.2 = (f32[5,16,1,384]{3,1,2,0:T(8,128)}, f32[5,16,1,384]{3,1,2,0:T(8,128)}, u32[]{:S(2)}, u32[]{:S(2)}) collective-permute-start(f32[5,16,1,384]{3,1,2,0:T(8,128)} %copy.59), channel_id=1, source_target_pairs={{0,1},{1,2},{2,3},{3,4},{4,5},{5,6},{6,7},{8,9},{9,10},{10,11},{11... | collective-permute-start | bytes 368648 | tf_op jit(solution)/shard_map/ppermute | solution.py:17
  8.7 0.7 copy.61
  9.4 1.3 collective-permute-start.3
  10.7 1.3 pad_maximum_fusion.8
  12.0 2.4 copy.55
  14.3 0.5 copy.57
  14.8 1.8 collective-permute-start.1
  16.8 1.3 collective-permute-done
  18.1 1.3 copy.56
  19.4 2.2 multiply_bitcast_fusion.1
  21.6 1.0 fusion.7
  22.6 2.3 copy.58
  24.8 2.7 multiply_subtract_fusion
  27.6 1.0 copy.60
  28.9 1.0 copy.62
  30.0 1.2 subtract_select_fusion
  31.1 2.3 fusion.4
  33.4 3.8 %all-to-all-start = ((f32[4,384,384]{2,1,0:T(8,128)}), f32[4,384,384]{2,1,0:T(8,128)S(1)}, u32[]{:S(2)}, u32[]{:S(2)}) async-start(f32[4,384,384]{2,1,0:T(8,128)} %bitcast.64), calls=%async_computation | async-start | bytes 4718592 | tf_op jit(solution)/shard_map/all_to_all | solution.py:71
  37.2 0.7 fusion.24
  37.9 1.6 fusion.14
  39.5 5.8 %add_select_fusion = f32[24,64,1536]{2,1,0:T(8,128)} fusion(f32[64,1536]{1,0:T(8,128)S(1)} %get-tuple-element.29, f32[24,1536]{1,0:T(8,128)S(1)} %get-tuple-element.19, f32[64,1536]{1,0:T(8,128)S(1)} %get-tuple-element.28, f32[24,1536]{1,0:T(8,128)S(1)} %get-tuple-element.18, pred[1536]{0:T(1024)(128)(4,1)S(1)} %iota_compare_fusion.4), kind=kLoop, calls=%fused_computation.2 | loop fusion | flops 16515072 | bytes 10520064 | tf_op jit(solution)/shard_map/jit(_where)/select_n | solution.py:62
  45.3 20.2 %all-to-all-done = f32[4,384,384]{2,1,0:T(8,128)S(1)} async-done(((f32[4,384,384]{2,1,0:T(8,128)}), f32[4,384,384]{2,1,0:T(8,128)S(1)}, u32[]{:S(2)}, u32[]{:S(2)}) %all-to-all-start) | async-done | bytes 2359328 | tf_op jit(solution)/shard_map/all_to_all | solution.py:71
  65.5 2.9 copy.63
  68.5 2.7 dot_general.8
  71.2 14.7 %convolution_multiply_fusion = f32[16,24,1536]{2,1,0:T(8,128)S(1)} fusion(f32[16,24,1536]{2,1,0:T(8,128)S(1)} %dot_general.8, f32[1536,1536,1]{1,0,2:T(8,128)} %bitcast.60, f32[24,1536]{1,0:T(8,128)S(1)} %fusion.18), kind=kOutput, calls=%fused_computation.13 | convolution fusion | flops 10872225792 | bytes 14303232 | tf_op jit(solution)/shard_map/dot_general | solution.py:73
  85.9 13.0 %fusion.31 = f32[384,4,384]{2,0,1:T(8,128)} fusion(f32[384,1536,1]{1,0,2:T(8,128)S(1)} %bitcast.67, f32[4,384,1536]{2,1,0:T(8,128)S(1)} %bitcast.61), kind=kOutput, calls=%fused_computation.95 | convolution fusion | flops 10871635968 | bytes 14155776 | tf_op jit(solution)/shard_map/dot_general | solution.py:79
  98.9 4.9 %all-to-all-start.1 = ((f32[384,4,384]{2,0,1:T(8,128)}), f32[384,4,384]{2,0,1:T(8,128)}, u32[]{:S(2)}, u32[]{:S(2)}) async-start(f32[384,4,384]{2,0,1:T(8,128)} %fusion.31), calls=%async_computation.1 | async-start | bytes 4718592 | tf_op jit(solution)/shard_map/all_to_all | solution.py:80
  104.5 0.3 select_reduce_fusion
  104.9 2.7 collective-permute-start.4
  107.5 0.9 collective-permute-start.5
  108.5 0.8 collective-permute-start.6
  109.3 3.0 collective-permute-start.7
  112.3 1.0 collective-permute-start.8
  113.5 2.1 copy.80
  115.7 3.6 %collective-permute-start.9 = (s32[1,12]{0,1:T(8,128)S(1)}, s32[1,12]{0,1:T(8,128)S(1)}, u32[]{:S(2)}, u32[]{:S(2)}) collective-permute-start(s32[1,12]{0,1:T(8,128)S(1)} %get-tuple-element.21), channel_id=1, source_target_pairs={{0,6},{1,7},{2,4},{3,5},{4,2},{5,3},{6,0},{7,1},{8,14},{9,15},{10,... | collective-permute-start | bytes 152 | tf_op jit(solution)/shard_map/ppermute | solution.py:102
  119.4 0.3 collective-permute-start.10
  120.2 1.0 collective-permute-done.9
  121.3 4.5 %collective-permute-done.10 = s32[1,12]{0,1:T(8,128)S(1)} collective-permute-done((s32[1,12]{0,1:T(8,128)S(1)}, s32[1,12]{0,1:T(8,128)S(1)}, u32[]{:S(2)}, u32[]{:S(2)}) %collective-permute-start.10) | collective-permute-done | bytes 80 | tf_op jit(solution)/shard_map/ppermute | solution.py:102
  126.0 4.8 %gather_fusion = f32[96,4,16,384]{3,2,1,0:T(8,128)} fusion(f32[24,4,16,384]{3,2,1,0:T(8,128)S(1)} %bitcast.62, s32[1024]{0:T(1024)S(1)} %pad_clamp_fusion.1), kind=kCustom, calls=%fused_computation | custom fusion | bytes 18874752 | tf_op jit(solution)/shard_map/gather | solution.py:125
  130.8 1.3 all-to-all-done.1
  132.1 7.1 %all-to-all-start.2 = ((f32[8,12,4,16,384]{4,3,2,1,0:T(8,128)}), f32[8,12,4,16,384]{4,3,2,1,0:T(8,128)}, u32[]{:S(2)}, u32[]{:S(2)}) async-start(f32[8,12,4,16,384]{4,3,2,1,0:T(8,128)} %bitcast.63), calls=%async_computation.2 | async-start | bytes 18874368 | tf_op jit(solution)/shard_map/all_to_all | solution.py:126
  139.4 3.3 add.159
  142.7 201.9 %all-to-all-done.2 = f32[8,12,4,16,384]{4,3,2,1,0:T(8,128)} async-done(((f32[8,12,4,16,384]{4,3,2,1,0:T(8,128)}), f32[8,12,4,16,384]{4,3,2,1,0:T(8,128)}, u32[]{:S(2)}, u32[]{:S(2)}) %all-to-all-start.2) | async-done | bytes 9437216 | tf_op jit(solution)/shard_map/all_to_all | solution.py:126
  344.6 6.7 %gather_fusion.1 = f32[48,4,16,384]{3,2,1,0:T(8,128)} fusion(f32[96,4,16,384]{3,2,1,0:T(8,128)} %bitcast.18, s32[1024]{0:T(1024)S(1)} %pad_clamp_fusion), kind=kCustom, calls=%fused_computation.1 | custom fusion | bytes 9437376 | tf_op jit(solution)/shard_map/gather | solution.py:128
  351.4 2.9 fusion.2
  354.3 2.8 copy.77
  (71 shorter events, 2.3 us)
Async XLA Ops:
  0.6 10.0 %copy-start = (f32[4,16,24,384]{3,2,1,0:T(8,128)S(1)}, f32[4,16,24,384]{3,2,1,0:T(8,128)}, u32[]{:S(2)}) copy-start(f32[4,16,24,384]{3,2,1,0:T(8,128)} %param.8) | copy-start | bytes 7077892
  0.6 10.0 %copy-start.3 = (f32[16,24,384]{2,1,0:T(8,128)S(1)}, f32[16,24,384]{2,1,0:T(8,128)}, u32[]{:S(2)}) copy-start(f32[16,24,384]{2,1,0:T(8,128)} %param.10) | copy-start | bytes 1769476
  3.2 24.4 %collective-permute-start.2 = (f32[5,16,1,384]{3,1,2,0:T(8,128)}, f32[5,16,1,384]{3,1,2,0:T(8,128)}, u32[]{:S(2)}, u32[]{:S(2)}) collective-permute-start(f32[5,16,1,384]{3,1,2,0:T(8,128)} %copy.59), channel_id=1, source_target_pairs={{0,1},{1,2},{2,3},{3,4},{4,5},{5,6},{6,7},{8,9},{9,10},{10,11},{11... | collective-permute-start | bytes 368648 | tf_op jit(solution)/shard_map/ppermute | solution.py:17
  9.4 19.6 %collective-permute-start.3 = (f32[5,16,1,384]{3,1,2,0:T(8,128)}, f32[5,16,1,384]{3,1,2,0:T(8,128)}, u32[]{:S(2)}, u32[]{:S(2)}) collective-permute-start(f32[5,16,1,384]{3,1,2,0:T(8,128)} %copy.61), channel_id=1, source_target_pairs={{1,0},{2,1},{3,2},{4,3},{5,4},{6,5},{7,6},{9,8},{10,9},{11,10},{12... | collective-permute-start | bytes 368648 | tf_op jit(solution)/shard_map/ppermute | solution.py:18
  10.7 6.0 %copy-start.8 = (s32[24]{0:T(128)S(1)}, s32[24]{0:T(128)}, u32[]{:S(2)}) copy-start(s32[24]{0:T(128)} %param.12) | copy-start | bytes 292
  14.3 3.7 %collective-permute-start = (f32[5,16,24,1]{2,1,3,0:T(8,128)}, f32[5,16,24,1]{2,1,3,0:T(8,128)}, u32[]{:S(2)}, u32[]{:S(2)}) collective-permute-start(f32[5,16,24,1]{2,1,3,0:T(8,128)} %copy.55), channel_id=1, source_target_pairs={{0,8},{8,16},{16,24},{24,0},{1,9},{9,17},{17,25},{25,1},{2,10},{10... | collective-permute-start | bytes 23048 | tf_op jit(solution)/shard_map/ppermute | solution.py:17
  14.8 7.7 %collective-permute-start.1 = (f32[5,16,24,1]{2,1,3,0:T(8,128)S(1)}, f32[5,16,24,1]{2,1,3,0:T(8,128)}, u32[]{:S(2)}, u32[]{:S(2)}) collective-permute-start(f32[5,16,24,1]{2,1,3,0:T(8,128)S(1)} %copy.57), channel_id=1, source_target_pairs={{8,0},{16,8},{24,16},{0,24},{9,1},{17,9},{25,17},{1,25},{10,2},{18... | collective-permute-start | bytes 23048 | tf_op jit(solution)/shard_map/ppermute | solution.py:18
  24.8 3.8 %copy-start.4 = (f32[16,24,384]{2,1,0:T(8,128)S(1)}, f32[16,24,384]{2,1,0:T(8,128)}, u32[]{:S(2)}) copy-start(f32[16,24,384]{2,1,0:T(8,128)} %param.11) | copy-start | bytes 1769476
  33.4 32.1 %all-to-all-start = ((f32[4,384,384]{2,1,0:T(8,128)}), f32[4,384,384]{2,1,0:T(8,128)S(1)}, u32[]{:S(2)}, u32[]{:S(2)}) async-start(f32[4,384,384]{2,1,0:T(8,128)} %bitcast.64), calls=%async_computation | async-start | bytes 4718592 | tf_op jit(solution)/shard_map/all_to_all | solution.py:71
  71.2 14.8 %copy-start.1 = (f32[24,64,1536]{2,1,0:T(8,128)S(1)}, f32[24,64,1536]{2,1,0:T(8,128)}, u32[]{:S(2)}) copy-start(f32[24,64,1536]{2,1,0:T(8,128)} %add_select_fusion) | copy-start | bytes 28311556
  98.9 5.0 %copy-start.5 = (s32[24,2]{0,1:T(2,128)S(1)}, s32[24,2]{0,1:T(2,128)}, u32[]{:S(2)}) copy-start(s32[24,2]{0,1:T(2,128)} %param.13) | copy-start | bytes 580
  98.9 5.1 %copy-start.7 = (s32[24,2]{0,1:T(2,128)S(1)}, s32[24,2]{0,1:T(2,128)}, u32[]{:S(2)}) copy-start(s32[24,2]{0,1:T(2,128)} %param.14) | copy-start | bytes 580
  98.9 33.2 %all-to-all-start.1 = ((f32[384,4,384]{2,0,1:T(8,128)}), f32[384,4,384]{2,0,1:T(8,128)}, u32[]{:S(2)}, u32[]{:S(2)}) async-start(f32[384,4,384]{2,0,1:T(8,128)} %fusion.31), calls=%async_computation.1 | async-start | bytes 4718592 | tf_op jit(solution)/shard_map/all_to_all | solution.py:80
  104.9 10.8 %collective-permute-start.4 = (s32[1,12]{0,1:T(8,128)S(1)}, s32[1,12]{0,1:T(8,128)S(1)}, u32[]{:S(2)}, u32[]{:S(2)}) collective-permute-start(s32[1,12]{0,1:T(8,128)S(1)} %get-tuple-element.26), channel_id=1, source_target_pairs={{0,1},{1,0},{2,3},{3,2},{4,5},{5,4},{6,7},{7,6},{8,9},{9,8},{10,11... | collective-permute-start | bytes 152 | tf_op jit(solution)/shard_map/ppermute | solution.py:102
  107.5 11.9 %collective-permute-start.5 = (s32[1,12]{0,1:T(8,128)S(1)}, s32[1,12]{0,1:T(8,128)S(1)}, u32[]{:S(2)}, u32[]{:S(2)}) collective-permute-start(s32[1,12]{0,1:T(8,128)S(1)} %get-tuple-element.25), channel_id=1, source_target_pairs={{0,2},{1,3},{2,0},{3,1},{4,6},{5,7},{6,4},{7,5},{8,10},{9,11},{10,... | collective-permute-start | bytes 152 | tf_op jit(solution)/shard_map/ppermute | solution.py:102
  108.5 11.4 %collective-permute-start.6 = (s32[1,12]{0,1:T(8,128)S(1)}, s32[1,12]{0,1:T(8,128)S(1)}, u32[]{:S(2)}, u32[]{:S(2)}) collective-permute-start(s32[1,12]{0,1:T(8,128)S(1)} %get-tuple-element.24), channel_id=1, source_target_pairs={{0,3},{1,2},{2,1},{3,0},{4,7},{5,6},{6,5},{7,4},{8,11},{9,10},{10,... | collective-permute-start | bytes 152 | tf_op jit(solution)/shard_map/ppermute | solution.py:102
  109.3 10.6 %collective-permute-start.7 = (s32[1,12]{0,1:T(8,128)S(1)}, s32[1,12]{0,1:T(8,128)S(1)}, u32[]{:S(2)}, u32[]{:S(2)}) collective-permute-start(s32[1,12]{0,1:T(8,128)S(1)} %get-tuple-element.23), channel_id=1, source_target_pairs={{0,4},{1,5},{2,6},{3,7},{4,0},{5,1},{6,2},{7,3},{8,12},{9,13},{10,... | collective-permute-start | bytes 152 | tf_op jit(solution)/shard_map/ppermute | solution.py:102
  112.3 7.7 %collective-permute-start.8 = (s32[1,12]{0,1:T(8,128)S(1)}, s32[1,12]{0,1:T(8,128)S(1)}, u32[]{:S(2)}, u32[]{:S(2)}) collective-permute-start(s32[1,12]{0,1:T(8,128)S(1)} %get-tuple-element.22), channel_id=1, source_target_pairs={{0,5},{1,4},{2,7},{3,6},{4,1},{5,0},{6,3},{7,2},{8,13},{9,12},{10,... | collective-permute-start | bytes 152 | tf_op jit(solution)/shard_map/ppermute | solution.py:102
  115.7 5.5 %collective-permute-start.9 = (s32[1,12]{0,1:T(8,128)S(1)}, s32[1,12]{0,1:T(8,128)S(1)}, u32[]{:S(2)}, u32[]{:S(2)}) collective-permute-start(s32[1,12]{0,1:T(8,128)S(1)} %get-tuple-element.21), channel_id=1, source_target_pairs={{0,6},{1,7},{2,4},{3,5},{4,2},{5,3},{6,0},{7,1},{8,14},{9,15},{10,... | collective-permute-start | bytes 152 | tf_op jit(solution)/shard_map/ppermute | solution.py:102
  119.4 6.4 %collective-permute-start.10 = (s32[1,12]{0,1:T(8,128)S(1)}, s32[1,12]{0,1:T(8,128)S(1)}, u32[]{:S(2)}, u32[]{:S(2)}) collective-permute-start(s32[1,12]{0,1:T(8,128)S(1)} %get-tuple-element.20), channel_id=1, source_target_pairs={{0,7},{1,6},{2,5},{3,4},{4,3},{5,2},{6,1},{7,0},{8,15},{9,14},{10,... | collective-permute-start | bytes 152 | tf_op jit(solution)/shard_map/ppermute | solution.py:102
  132.1 7.3 %copy-start.6 = (f32[24,2]{0,1:T(2,128)S(1)}, f32[24,2]{0,1:T(2,128)}, u32[]{:S(2)}) copy-start(f32[24,2]{0,1:T(2,128)} %param.15) | copy-start | bytes 580
  132.1 7.3 %copy-start.2 = (f32[4,16,24,384]{3,2,1,0:T(8,128)S(1)}, f32[4,16,24,384]{3,2,1,0:T(8,128)}, u32[]{:S(2)}) copy-start(f32[4,16,24,384]{3,2,1,0:T(8,128)} %fusion.4) | copy-start | bytes 7077892
  132.1 212.5 %all-to-all-start.2 = ((f32[8,12,4,16,384]{4,3,2,1,0:T(8,128)}), f32[8,12,4,16,384]{4,3,2,1,0:T(8,128)}, u32[]{:S(2)}, u32[]{:S(2)}) async-start(f32[8,12,4,16,384]{4,3,2,1,0:T(8,128)} %bitcast.63), calls=%async_computation.2 | async-start | bytes 18874368 | tf_op jit(solution)/shard_map/all_to_all | solution.py:126
